TPU v7x, 256 devices: a whole 4x4x8 slice. The times are simulated.
256 devices in a mesh: pix: 32 (over z, x), feat: 8 (over y, core).
Axes of the slice: x: 4, y: 4, z: 8, core: 2. Of those that a mesh axis runs over, the one named last changes fastest.
Arguments:
- mass_bin: int32 [262144, 256], P(('pix', 'feat')), may hold values from 0 to 255
- mobility_bin: int32 [262144, 256], P(('pix', 'feat')), may hold values from 0 to 15
- intensity: bfloat16 [262144, 256], P(('pix', 'feat')), may hold values from 10 to 4000, as said below
- basis_init: float32 [262144, 64], P(('pix', 'feat')), may hold values from 0.1 to 1
- profile_init: float32 [64, 4096], P(None, 'feat'), may hold values from 0.1 to 1
Outputs:
- basis: float32 [262144, 64], P(('pix', 'feat'))
- profiles: float32 [64, 4096], P(None, 'feat')
Inputs may be any that keep to these rules, and one draw needn't show every extreme that they name: `intensity`: positive peak intensities.
All inputs are finite; a program needn't handle non-finite values.
Results may differ from a plain program's by a relative error of at most 0.00045.
Values may be sent and summed in bfloat16 or wider, within the bound.
No kernel may reach another device: no remote copies, remote signals or barrier semaphores. Data moves between devices by JAX's collectives and lax.ppermute only.
A program may use at most 64 MiB of HBM per device.

v0:
```python
import math
import jax
import jax.numpy as jnp
from jax import lax
from jax.sharding import PartitionSpec as P

MZ = 256
MOB = 16
PEAKS = 256
ITERS = 2
EPS = 1e-06


def bin_block(args):
    mass, mobility, weight = args
    mass_hot = (mass[:, :, None] == jnp.arange(MZ, dtype=jnp.int32)[None, None, :]).astype(
        jnp.bfloat16
    ) * weight[:, :, None]
    mobility_hot = (mobility[:, :, None] == jnp.arange(MOB, dtype=jnp.int32)[None, None, :]).astype(
        jnp.bfloat16
    )
    dense = jnp.einsum("pkb,pkm->pbm", mobility_hot, mass_hot, preferred_element_type=jnp.float32)
    return dense.reshape(mass.shape[0], MZ * MOB).astype(jnp.bfloat16)


def local(mass_bin, mobility_bin, intensity, basis_init, profile_init):
    rows = mass_bin.shape[0]
    block = math.gcd(rows, 32)
    count = rows // block
    spectra = lax.map(
        bin_block,
        (
            mass_bin.reshape(count, block, PEAKS),
            mobility_bin.reshape(count, block, PEAKS),
            intensity.reshape(count, block, PEAKS),
        ),
    )
    spectra = spectra.reshape(rows, MZ * MOB)
    highest = lax.Precision.HIGHEST
    basis, profiles = (basis_init, profile_init)
    for step in range(ITERS):
        partial_h = lax.dot_general(
            basis.astype(jnp.bfloat16),
            spectra,
            (((0,), (0,)), ((), ())),
            preferred_element_type=jnp.float32,
        )
        partial_gram = lax.dot_general(
            basis,
            basis,
            (((0,), (0,)), ((), ())),
            precision=highest,
            preferred_element_type=jnp.float32,
        )
        shared = lax.psum_scatter(partial_h, "feat", scatter_dimension=1, tiled=True)
        numer_h = lax.psum(shared, "pix")
        gram_w = lax.psum(partial_gram, ("pix", "feat"))
        profiles = (
            profiles
            * numer_h
            / (
                jnp.dot(gram_w, profiles, precision=highest, preferred_element_type=jnp.float32)
                + EPS
            )
        )
        numer_w = lax.dot_general(
            spectra,
            lax.all_gather(profiles.astype(jnp.bfloat16), "feat", axis=1, tiled=True),
            (((1,), (1,)), ((), ())),
            preferred_element_type=jnp.float32,
        )
        local_gram = lax.dot_general(
            profiles,
            profiles,
            (((1,), (1,)), ((), ())),
            precision=highest,
            preferred_element_type=jnp.float32,
        )
        gram_h = lax.psum(local_gram, "feat")
        basis = (
            basis
            * numer_w
            / (jnp.dot(basis, gram_h, precision=highest, preferred_element_type=jnp.float32) + EPS)
        )
    return (basis, profiles)


def solution(mesh):
    return jax.shard_map(
        local,
        mesh=mesh,
        in_specs=(
            P(("pix", "feat"), None),
            P(("pix", "feat"), None),
            P(("pix", "feat"), None),
            P(("pix", "feat"), None),
            P(None, "feat"),
        ),
        out_specs=(P(("pix", "feat"), None), P(None, "feat")),
        check_vma=False,
    )
```

profile of v0, /device:TPU:2, one launch (start us, length us, event | category | flops | bytes accessed | tf_op | source)
XLA Modules:
  0.0 668.2 jit_solution(15157433333801755827)
XLA Ops:
  7.2 192.9 %while.10 = (s32[]{:T(128)}, bf16[32,32,4096]{2,1,0:T(8,128)(2,1)}, s32[32,32,256]{2,1,0:T(8,128)}, s32[32,32,256]{2,1,0:T(8,128)}, bf16[32,32,256]{2,1,0:T(8,128)(2,1)}, /*index=5*/s32[]{:T(128)}) while((s32[]{:T(128)}, bf16[32,32,4096]{2,1,0:T(8,128)(2,1)}, s32[32,32,256]{2,1,0:T(8,128)}, s32[32,32,256]{2,1,0:T(8,128)}, ...), condition=%wide.region_1.2_spmd, body=%wide.region_0.1_spmd.sunk | while | flops 71565312 | bytes 1557069 | solution.py:30
  8.8 3.7 fusion.50
  14.8 3.7 fusion.50
  20.8 3.7 fusion.50
  26.8 3.7 fusion.50
  32.9 3.7 fusion.50
  38.9 3.7 fusion.50
  44.9 3.7 fusion.50
  51.0 3.7 fusion.50
  57.0 3.7 fusion.50
  63.0 3.7 fusion.50
  69.0 3.7 fusion.50
  75.1 3.7 fusion.50
  81.1 3.7 fusion.50
  87.1 3.7 fusion.50
  93.2 3.7 fusion.50
  99.2 3.7 fusion.50
  105.2 3.7 fusion.50
  200.1 6.1 convolution_bitcast_fusion
  206.2 37.5 %reduce-scatter.3.cloned.1.call-done = f32[64,512]{1,0:T(8,128)} async-done(((f32[64,4096]{1,0:T(8,128)}), f32[64,512]{1,0:T(8,128)}) %reduce-scatter.3.cloned.1.call-update) | async-done | bytes 131088 | tf_op jit(solution)/shard_map/reduce_scatter | solution.py:55
  244.2 74.5 %psum.43 = f32[64,64]{1,0:T(8,128)S(1)} all-reduce(f32[64,64]{1,0:T(8,128)S(1)} %fusion.21), channel_id=1, replica_groups=mesh['pix'=32,'feat'=8] {'pix','feat'}, use_global_device_ids=true, to_apply=%region_4.5 | all-reduce | flops 4096 | bytes 32768 | tf_op jit(solution)/shard_map/psum | solution.py:57
  318.7 68.1 %all-reduce.3.cloned.1.call-done = f32[64,512]{1,0:T(8,128)} async-done(((f32[64,512]{1,0:T(8,128)}), f32[64,512]{1,0:T(8,128)}) %all-reduce.3.cloned.1.call-update) | async-done | bytes 131088 | tf_op jit(solution)/shard_map/psum | solution.py:56
  388.0 13.5 %all_gather.6 = bf16[64,4096]{1,0:T(8,128)(2,1)S(1)} all-gather(bf16[64,512]{1,0:T(8,128)(2,1)S(1)} %get-tuple-element.42), channel_id=1, replica_groups=mesh['pix'=32,'feat'=8] {'feat'}, dimensions={1}, use_global_device_ids=true | all-gather | bytes 589824 | tf_op jit(solution)/shard_map/all_gather | solution.py:68
  401.5 6.0 convolution_multiply_fusion.1
  407.8 25.8 %psum.44 = f32[64,64]{1,0:T(8,128)S(1)} all-reduce(f32[64,64]{1,0:T(8,128)S(1)} %fusion.22), channel_id=1, replica_groups=mesh['pix'=32,'feat'=8] {'feat'}, use_global_device_ids=true, to_apply=%region_5.6 | all-reduce | flops 4096 | bytes 32768 | tf_op jit(solution)/shard_map/psum | solution.py:79
  434.0 6.0 fusion.16
  440.1 30.4 %reduce-scatter.5.cloned.1.call-done = f32[64,512]{1,0:T(8,128)} async-done(((f32[64,4096]{1,0:T(8,128)}), f32[64,512]{1,0:T(8,128)}) %reduce-scatter.5.cloned.1.call-update) | async-done | bytes 131088 | tf_op jit(solution)/shard_map/reduce_scatter | solution.py:55
  470.8 74.4 %psum.46 = f32[64,64]{1,0:T(8,128)S(1)} all-reduce(f32[64,64]{1,0:T(8,128)S(1)} %fusion.23), channel_id=1, replica_groups=mesh['pix'=32,'feat'=8] {'pix','feat'}, use_global_device_ids=true, to_apply=%region_8.9 | all-reduce | flops 4096 | bytes 32768 | tf_op jit(solution)/shard_map/psum | solution.py:57
  545.2 68.6 %all-reduce.5.cloned.1.call-done = f32[64,512]{1,0:T(8,128)} async-done(((f32[64,512]{1,0:T(8,128)}), f32[64,512]{1,0:T(8,128)}) %all-reduce.5.cloned.1.call-update) | async-done | bytes 131088 | tf_op jit(solution)/shard_map/psum | solution.py:56
  615.0 13.4 %all_gather.7 = bf16[64,4096]{1,0:T(8,128)(2,1)S(1)} all-gather(bf16[64,512]{1,0:T(8,128)(2,1)S(1)} %get-tuple-element.44), channel_id=1, replica_groups=mesh['pix'=32,'feat'=8] {'feat'}, dimensions={1}, use_global_device_ids=true | all-gather | bytes 589824 | tf_op jit(solution)/shard_map/all_gather | solution.py:68
  628.5 6.0 convolution_multiply_fusion
  634.8 25.8 %psum.47 = f32[64,64]{1,0:T(8,128)S(1)} all-reduce(f32[64,64]{1,0:T(8,128)S(1)} %fusion.24), channel_id=1, replica_groups=mesh['pix'=32,'feat'=8] {'feat'}, use_global_device_ids=true, to_apply=%region_9.10 | all-reduce | flops 4096 | bytes 32768 | tf_op jit(solution)/shard_map/psum | solution.py:79
  (166 shorter events, 135.7 us)
Async XLA Ops:
  7.2 236.6 %reduce-scatter.3.cloned.1.call-start = ((), (), s32[]{:S(2)}) async-start(), calls=%async_computation.2 | async-start | bytes 1179648 | tf_op jit(solution)/shard_map/reduce_scatter | solution.py:55
  7.2 192.9 %copy-start = (f32[1024,64]{0,1:T(8,128)S(1)}, f32[1024,64]{0,1:T(8,128)}, u32[]{:S(2)}) copy-start(f32[1024,64]{0,1:T(8,128)} %param.10) | copy-start | bytes 786436
  200.1 186.7 %copy-start.2 = (f32[64,512]{1,0:T(8,128)S(1)}, f32[64,512]{1,0:T(8,128)}, u32[]{:S(2)}) copy-start(f32[64,512]{1,0:T(8,128)} %param.11) | copy-start | bytes 393220
  206.2 180.6 %all-reduce.3.cloned.1.call-start = ((), (), s32[]{:S(2)}) async-start(), calls=%async_computation.3 | async-start | bytes 262144 | tf_op jit(solution)/shard_map/psum | solution.py:56
  243.8 226.7 %reduce-scatter.5.cloned.1.call-start = ((), (), s32[]{:S(2)}) async-start(), calls=%async_computation.4 | async-start | bytes 1179648 | tf_op jit(solution)/shard_map/reduce_scatter | solution.py:55
  440.0 173.8 %all-reduce.5.cloned.1.call-start = ((), (), s32[]{:S(2)}) async-start(), calls=%async_computation.5 | async-start | bytes 262144 | tf_op jit(solution)/shard_map/psum | solution.py:56
  615.0 46.7 %copy-start.1 = (f32[64,512]{1,0:T(8,128)}, f32[64,512]{1,0:T(8,128)S(1)}, u32[]{:S(2)}) copy-start(f32[64,512]{1,0:T(8,128)S(1)} %get-tuple-element.45) | copy-start | bytes 393220
Sparse Core Ops, SparseCore 0:
  206.3 37.3 reduce-scatter.2
  247.2 139.5 all-reduce.2
  440.1 30.2 reduce-scatter.4
  474.1 139.6 all-reduce.4
where the time goes:
time: 673 us; the launch traced here: 668 us
  blocking collectives  227 us (34%)
  waiting for transfers between devices  205 us (30%)
  matrix products  146 us (22%)
  local copies, waits for them, and re-layouts  75.5 us (11%)
  between operations  13.8 us (2%)
    psum x2, blocking collectives, local(): gram_w = lax.psum(partial_gram, ('pix', 'feat'))  149 us
    psum x2, waiting for transfers between devices, local(): numer_h = lax.psum(shared, 'pix')  137 us
    dot_general x32, matrix products, bin_block(): jnp.einsum('pkb,pkm->pbm', mobility_hot, mass_hot, preferred_element_type...  117 us
    reduce_scatter x2, waiting for transfers between devices, local(): lax.psum_scatter(partial_h, 'feat', scatter_dimension=1, tiled=True)  67.8 us
    psum x2, blocking collectives, local(): gram_h = lax.psum(local_gram, 'feat')  51.6 us
    all_gather x2, blocking collectives, local(): lax.all_gather(profiles.astype(jnp.bfloat16), 'feat', axis=1, tiled=True)  26.9 us
    eq x32, local copies, waits for them, and re-layouts, bin_block(): mass[:, :, None] == jnp.arange(MZ, dtype=jnp.int32)[None, None, :]  25 us
    dynamic_update_slice x32, local copies, waits for them, and re-layouts, local(): lax.map(bin_block, (mass_bin.reshape(count, block, PEAKS), mobility_bin.r...  23.4 us
  transfers between devices with their start and end apart: 4, of which 4 were waited for; matrix products, arithmetic and copies ran while one was open for 0% of the time, Pallas kernels for 0%

commit v1 on v0

--- a/solution.py
+++ b/solution.py
@@ -1,3 +1,4 @@
+import functools
 import math
 import jax
 import jax.numpy as jnp
@@ -9,6 +10,13 @@
 PEAKS = 256
 ITERS = 2
 EPS = 1e-06
+
+
+def shape_words_by_axis(matrix, mesh_ax):
+    return jnp.sum(lax.all_gather(matrix, mesh_ax), axis=0)
+
+
+load_cycles = functools.partial(shape_words_by_axis, mesh_ax="pix")
 
 
 def bin_block(args):
@@ -53,7 +61,7 @@
             preferred_element_type=jnp.float32,
         )
         shared = lax.psum_scatter(partial_h, "feat", scatter_dimension=1, tiled=True)
-        numer_h = lax.psum(shared, "pix")
+        numer_h = load_cycles(shared)
         gram_w = lax.psum(partial_gram, ("pix", "feat"))
         profiles = (
             profiles

time: 673 us -> 555 us (0.82)
  waiting for transfers between devices: 205 us -> 82 us
    psum x2 -> x0, waiting for transfers between devices: 137 us -> none  [local(): numer_h = lax.psum(shared, 'pix')]
    all_gather x0 -> x2, waiting for transfers between devices: none -> 13.9 us  [shape_words_by_axis(): return jnp.sum(lax.all_gather(matrix, mesh_ax), axis=0)]
where the time goes in v1:
time: 555 us; the launch traced here: 550 us
  blocking collectives  228 us (41%)
  matrix products  145 us (26%)
  waiting for transfers between devices  82 us (15%)
  local copies, waits for them, and re-layouts  75.5 us (14%)
  between operations  13.9 us (3%)
    psum x2, blocking collectives, local(): gram_w = lax.psum(partial_gram, ('pix', 'feat'))  149 us
    dot_general x32, matrix products, bin_block(): jnp.einsum('pkb,pkm->pbm', mobility_hot, mass_hot, preferred_element_type...  117 us
    reduce_scatter x2, waiting for transfers between devices, local(): lax.psum_scatter(partial_h, 'feat', scatter_dimension=1, tiled=True)  68.1 us
    psum x2, blocking collectives, local(): gram_h = lax.psum(local_gram, 'feat')  51.6 us
    all_gather x2, blocking collectives, local(): lax.all_gather(profiles.astype(jnp.bfloat16), 'feat', axis=1, tiled=True)  27.1 us
    eq x32, local copies, waits for them, and re-layouts, bin_block(): mass[:, :, None] == jnp.arange(MZ, dtype=jnp.int32)[None, None, :]  25 us
    dynamic_update_slice x32, local copies, waits for them, and re-layouts, local(): lax.map(bin_block, (mass_bin.reshape(count, block, PEAKS), mobility_bin.r...  23.4 us
    mul x32, local copies, waits for them, and re-layouts, bin_block(): (mass[:, :, None] == jnp.arange(MZ, dtype=jnp.int32)[None, None, :]).asty...  23 us
  transfers between devices with their start and end apart: 4, of which 4 were waited for; matrix products, arithmetic and copies ran while one was open for 0% of the time, Pallas kernels for 0%

profile of v1, /device:TPU:2, one launch (start us, length us, event | category | flops | bytes accessed | tf_op | source)
XLA Modules:
  0.0 549.5 jit_solution(4222541035810572901)
XLA Ops:
  7.2 192.9 %while.10 = (s32[]{:T(128)}, bf16[32,32,4096]{2,1,0:T(8,128)(2,1)}, s32[32,32,256]{2,1,0:T(8,128)}, s32[32,32,256]{2,1,0:T(8,128)}, bf16[32,32,256]{2,1,0:T(8,128)(2,1)}, /*index=5*/s32[]{:T(128)}) while((s32[]{:T(128)}, bf16[32,32,4096]{2,1,0:T(8,128)(2,1)}, s32[32,32,256]{2,1,0:T(8,128)}, s32[32,32,256]{2,1,0:T(8,128)}, ...), condition=%wide.region_1.2_spmd, body=%wide.region_0.1_spmd.sunk | while | flops 71565312 | bytes 1557069 | solution.py:38
  8.8 3.7 fusion.50
  14.8 3.7 fusion.50
  20.8 3.7 fusion.50
  26.8 3.7 fusion.50
  32.9 3.7 fusion.50
  38.9 3.7 fusion.50
  44.9 3.7 fusion.50
  51.0 3.7 fusion.50
  57.0 3.7 fusion.50
  63.0 3.7 fusion.50
  69.0 3.7 fusion.50
  75.1 3.7 fusion.50
  81.1 3.7 fusion.50
  87.1 3.7 fusion.50
  93.2 3.7 fusion.50
  99.2 3.7 fusion.50
  105.2 3.7 fusion.50
  200.1 6.1 %convolution_bitcast_fusion = f32[64,4096]{1,0:T(8,128)} fusion(bf16[1024,4096]{1,0:T(8,128)(2,1)} %bitcast.44, f32[1024,64]{0,1:T(8,128)S(1)} %copy-done), kind=kOutput, calls=%fused_computation.14 | convolution fusion | flops 536936448 | bytes 9699328 | tf_op jit(solution)/shard_map/dot_general | solution.py:50
  206.2 37.5 %reduce-scatter.3.cloned.1.call-done = f32[64,512]{1,0:T(8,128)} async-done(((f32[64,4096]{1,0:T(8,128)}), f32[64,512]{1,0:T(8,128)}) %reduce-scatter.3.cloned.1.call-update) | async-done | bytes 131088 | tf_op jit(solution)/shard_map/reduce_scatter | solution.py:63
  244.2 74.7 %psum.28 = f32[64,64]{1,0:T(8,128)S(1)} all-reduce(f32[64,64]{1,0:T(8,128)S(1)} %fusion.21), channel_id=1, replica_groups=mesh['pix'=32,'feat'=8] {'pix','feat'}, use_global_device_ids=true, to_apply=%region_4.5 | all-reduce | flops 4096 | bytes 32768 | tf_op jit(solution)/shard_map/psum | solution.py:65
  318.9 6.9 %all-gather.5.cloned.1.call-done = f32[2048,512]{1,0:T(8,128)} async-done(((f32[64,512]{1,0:T(8,128)}), f32[2048,512]{1,0:T(8,128)}) %all-gather.5.cloned.1.call-update) | async-done | bytes 4194320 | tf_op jit(solution)/shard_map/all_gather | solution.py:16
  328.6 13.5 %all_gather.20 = bf16[64,4096]{1,0:T(8,128)(2,1)S(1)} all-gather(bf16[64,512]{1,0:T(8,128)(2,1)S(1)} %get-tuple-element.42), channel_id=1, replica_groups=mesh['pix'=32,'feat'=8] {'feat'}, dimensions={1}, use_global_device_ids=true | all-gather | bytes 589824 | tf_op jit(solution)/shard_map/all_gather | solution.py:76
  342.1 6.0 %convolution_multiply_fusion.1 = f32[1024,64]{0,1:T(8,128)S(1)} fusion(f32[1024,64]{0,1:T(8,128)S(1)} %copy-done, bf16[1024,4096]{1,0:T(8,128)(2,1)} %bitcast.45, bf16[64,4096]{1,0:T(8,128)(2,1)S(1)} %all_gather.20), kind=kOutput, calls=%fused_computation.21 | convolution fusion | flops 536936448 | bytes 9437184 | tf_op jit(solution)/shard_map/dot_general | solution.py:74
  348.4 25.8 %psum.29 = f32[64,64]{1,0:T(8,128)S(1)} all-reduce(f32[64,64]{1,0:T(8,128)S(1)} %fusion.22), channel_id=1, replica_groups=mesh['pix'=32,'feat'=8] {'feat'}, use_global_device_ids=true, to_apply=%region_5.6 | all-reduce | flops 4096 | bytes 32768 | tf_op jit(solution)/shard_map/psum | solution.py:87
  374.6 6.0 %fusion.16 = f32[64,4096]{1,0:T(8,128)} fusion(bf16[1024,4096]{1,0:T(8,128)(2,1)} %bitcast.46, f32[1024,64]{0,1:T(8,128)S(1)} %fusion.13), kind=kOutput, calls=%fused_computation.26 | convolution fusion | flops 536936448 | bytes 9699328 | tf_op jit(solution)/shard_map/dot_general | solution.py:50
  380.7 30.6 %reduce-scatter.5.cloned.1.call-done = f32[64,512]{1,0:T(8,128)} async-done(((f32[64,4096]{1,0:T(8,128)}), f32[64,512]{1,0:T(8,128)}) %reduce-scatter.5.cloned.1.call-update) | async-done | bytes 131088 | tf_op jit(solution)/shard_map/reduce_scatter | solution.py:63
  411.7 74.6 %psum.30 = f32[64,64]{1,0:T(8,128)S(1)} all-reduce(f32[64,64]{1,0:T(8,128)S(1)} %fusion.23), channel_id=1, replica_groups=mesh['pix'=32,'feat'=8] {'pix','feat'}, use_global_device_ids=true, to_apply=%region_8.9 | all-reduce | flops 4096 | bytes 32768 | tf_op jit(solution)/shard_map/psum | solution.py:65
  486.3 6.9 %all-gather.7.cloned.1.call-done = f32[2048,512]{1,0:T(8,128)} async-done(((f32[64,512]{1,0:T(8,128)}), f32[2048,512]{1,0:T(8,128)}) %all-gather.7.cloned.1.call-update) | async-done | bytes 4194320 | tf_op jit(solution)/shard_map/all_gather | solution.py:16
  496.1 13.7 %all_gather.23 = bf16[64,4096]{1,0:T(8,128)(2,1)S(1)} all-gather(bf16[64,512]{1,0:T(8,128)(2,1)S(1)} %get-tuple-element.44), channel_id=1, replica_groups=mesh['pix'=32,'feat'=8] {'feat'}, dimensions={1}, use_global_device_ids=true | all-gather | bytes 589824 | tf_op jit(solution)/shard_map/all_gather | solution.py:76
  509.8 6.0 %convolution_multiply_fusion = f32[1024,64]{0,1:T(8,128)S(1)} fusion(f32[1024,64]{0,1:T(8,128)S(1)} %fusion.13, bf16[1024,4096]{1,0:T(8,128)(2,1)} %bitcast.47, bf16[64,4096]{1,0:T(8,128)(2,1)S(1)} %all_gather.23), kind=kOutput, calls=%fused_computation.20 | convolution fusion | flops 536936448 | bytes 9437184 | tf_op jit(solution)/shard_map/dot_general | solution.py:74
  516.1 25.8 %psum.31 = f32[64,64]{1,0:T(8,128)S(1)} all-reduce(f32[64,64]{1,0:T(8,128)S(1)} %fusion.24), channel_id=1, replica_groups=mesh['pix'=32,'feat'=8] {'feat'}, use_global_device_ids=true, to_apply=%region_9.10 | all-reduce | flops 4096 | bytes 32768 | tf_op jit(solution)/shard_map/psum | solution.py:87
  (168 shorter events, 139.0 us)
Async XLA Ops:
  7.2 236.6 %reduce-scatter.3.cloned.1.call-start = ((), (), s32[]{:S(2)}) async-start(), calls=%async_computation.2 | async-start | bytes 1179648 | tf_op jit(solution)/shard_map/reduce_scatter | solution.py:63
  7.2 192.9 %copy-start = (f32[1024,64]{0,1:T(8,128)S(1)}, f32[1024,64]{0,1:T(8,128)}, u32[]{:S(2)}) copy-start(f32[1024,64]{0,1:T(8,128)} %param.10) | copy-start | bytes 786436
  200.1 128.2 %copy-start.2 = (f32[64,512]{1,0:T(8,128)S(1)}, f32[64,512]{1,0:T(8,128)}, u32[]{:S(2)}) copy-start(f32[64,512]{1,0:T(8,128)} %param.11) | copy-start | bytes 393220
  206.2 119.6 %all-gather.5.cloned.1.call-start = ((), (), s32[]{:S(2)}) async-start(), calls=%async_computation.4 | async-start | bytes 4325376 | tf_op jit(solution)/shard_map/all_gather | solution.py:16
  243.8 167.6 %reduce-scatter.5.cloned.1.call-start = ((), (), s32[]{:S(2)}) async-start(), calls=%async_computation.3 | async-start | bytes 1179648 | tf_op jit(solution)/shard_map/reduce_scatter | solution.py:63
  380.6 112.6 %all-gather.7.cloned.1.call-start = ((), (), s32[]{:S(2)}) async-start(), calls=%async_computation.5 | async-start | bytes 4325376 | tf_op jit(solution)/shard_map/all_gather | solution.py:16
  496.1 46.9 %copy-start.1 = (f32[64,512]{1,0:T(8,128)}, f32[64,512]{1,0:T(8,128)S(1)}, u32[]{:S(2)}) copy-start(f32[64,512]{1,0:T(8,128)S(1)} %get-tuple-element.45) | copy-start | bytes 393220
Sparse Core Ops, SparseCore 0:
  206.3 37.3 reduce-scatter.2
  246.3 79.4 all-gather.4
  380.8 30.5 reduce-scatter.4
  413.8 79.4 all-gather.6
